TPU v7x, 256 devices: a whole 4x4x8 slice. The times are simulated.
256 devices in a mesh: dp: 16 (over z_lo, y, core), ctx: 16 (over x, z_hi).
Axes of the slice: x: 4, y: 4, z: 8 (z_hi: 4, z_lo: 2; z = z_hi * 2 + z_lo), core: 2. Of those that a mesh axis runs over, the one named last changes fastest.
Arguments:
- tokens: bfloat16 [16, 2048, 2560], P('dp', 'ctx'), may hold values from -6 to 6
- shard_counts: int32 [16, 16], P('dp'), may hold values from 64 to 128, as said below
- stretch_start: int32 [16], P('dp'), may hold values from 102 to 409, as said below
- segment_ids: int32 [16, 2048], P('dp', 'ctx'), may hold values from 0 to 1, as said below
- span_ids: int32 [16, 2048], P('dp', 'ctx'), may hold values from -1 to 31, as said below
- query_weight: bfloat16 [2560, 2560], P('dp'), may hold values from -0.125 to 0.125
- key_matrix: bfloat16 [2560, 512], P('dp'), may hold values from -0.125 to 0.125
- value_matrix: bfloat16 [2560, 512], P('dp'), may hold values from -0.125 to 0.125
- score_vector: bfloat16 [2560], replicated, may hold values from -4 to 4
Outputs:
- attention: bfloat16 [16, 2048, 2560], P('dp', 'ctx')
- candidate_loglik: float32 [16, 32], P('dp')
Inputs may be any that keep to these rules, and one draw needn't show every extreme that they name: `shard_counts`: in every sequence at least one shard has exactly 128 live tokens. `stretch_start`: A stretch of each sequence starts at a position held by one of its live tokens, after the first. `segment_ids`: along the live tokens of a sequence, segment ids never fall. `span_ids`: each candidate of every sequence covers one or more live tokens, in one run of consecutive positions; empty slots have -1.
All inputs are finite; a program needn't handle non-finite values.
Results may differ from a plain program's by a relative error of at most 0.0066.
Values may be sent and summed in bfloat16 or wider, within the bound.
No kernel may reach another device: no remote copies, remote signals or barrier semaphores. Data moves between devices by JAX's collectives and lax.ppermute only.
A program may use at most 128 MiB of HBM per device.

v0:
```python
import math
import jax
import jax.numpy as jnp
from jax import lax
from jax.sharding import PartitionSpec as P

QUERY_HEADS = 20
KEY_VALUE_HEADS = 4
HEAD_SIZE = 128
STRETCH = 8192
CAND = 32
THETA = 500000.0
EPS = 1e-05


def rotary_then_norm(value_rows, token_places, heads):
    token_count = value_rows.shape[0]
    half = HEAD_SIZE // 2
    shaped = value_rows.reshape(token_count, heads, HEAD_SIZE)
    freqs = jnp.exp(jnp.arange(half, dtype=jnp.float32) * (-2.0 * math.log(THETA) / HEAD_SIZE))
    angles = token_places.astype(jnp.float32)[:, None] * freqs[None, :]
    cosine = jnp.cos(angles)[:, None, :]
    sine = jnp.sin(angles)[:, None, :]
    leading_block = shaped[..., :half]
    second = shaped[..., half:]
    turned = jnp.concatenate(
        [leading_block * cosine - second * sine, second * cosine + leading_block * sine], axis=-1
    )
    scale = lax.rsqrt(jnp.mean(turned * turned, axis=-1, keepdims=True) + EPS)
    return (turned * scale).astype(jnp.bfloat16).reshape(token_count, heads * HEAD_SIZE)


def per_device(
    tokens,
    shard_counts,
    stretch_start,
    segment_ids,
    span_ids,
    query_weight,
    key_matrix,
    value_matrix,
    score_vector,
):
    inputs = tokens[0]
    token_slots = inputs.shape[0]
    shards = lax.axis_size("ctx")
    mine = lax.axis_index("ctx")
    counts = shard_counts[0]
    order = jnp.arange(shards, dtype=jnp.int32)
    count_mine = jnp.sum(jnp.where(order == mine, counts, 0))
    start_mine = jnp.sum(jnp.where(order < mine, counts, 0))
    offsets = jnp.arange(token_slots, dtype=jnp.int32)
    token_places = start_mine + offsets
    live = offsets < count_mine
    cstart = stretch_start[0]
    qseg = segment_ids[0]
    qchunk = (token_places + STRETCH - cstart) // STRETCH
    pieces = (
        lax.all_gather(query_weight, "dp", axis=0, tiled=True),
        lax.all_gather(key_matrix, "dp", axis=0, tiled=True),
        lax.all_gather(value_matrix, "dp", axis=0, tiled=True),
    )
    query, key_rows, raw_values = tuple(
        (jnp.dot(inputs, piece, preferred_element_type=jnp.float32) for piece in pieces)
    )
    value_rows = raw_values.astype(jnp.bfloat16)
    query_norm = rotary_then_norm(query, token_places, QUERY_HEADS)
    key_norm = rotary_then_norm(key_rows, token_places, KEY_VALUE_HEADS)
    kplace = jnp.where(live, token_places + 1, 0)
    head_group = QUERY_HEADS // KEY_VALUE_HEADS
    per_head_queries = query_norm.reshape(token_slots, KEY_VALUE_HEADS, head_group, HEAD_SIZE)

    def add_keys(piece):
        key_portion, value_portion, kpos, kseg = piece
        token_count = key_portion.shape[0]
        kchunk = (kpos - 1 + STRETCH - cstart) // STRETCH
        scores = jnp.einsum(
            "qhgd,khd->hgqk",
            per_head_queries,
            key_portion.reshape(token_count, KEY_VALUE_HEADS, HEAD_SIZE),
            preferred_element_type=jnp.float32,
        ) * (1.0 / math.sqrt(HEAD_SIZE))
        allowed = (kseg[None, :] == qseg[:, None]) & (kchunk[None, :] == qchunk[:, None])
        allowed = allowed & (kpos[None, :] >= 1) & (kpos[None, :] <= token_places[:, None] + 1)
        weights = jnp.where(allowed[None, None], jnp.exp(scores), 0.0)
        denom = jnp.sum(weights, axis=-1)
        numer = jnp.einsum(
            "hgqk,khd->qhgd",
            weights.astype(jnp.bfloat16),
            value_portion.reshape(token_count, KEY_VALUE_HEADS, HEAD_SIZE),
            preferred_element_type=jnp.float32,
        )
        return (numer, denom)

    empty = (
        jnp.zeros((token_slots, KEY_VALUE_HEADS, head_group, HEAD_SIZE), jnp.float32),
        jnp.zeros((KEY_VALUE_HEADS, head_group, token_slots), jnp.float32),
    )
    own_block = (key_norm, value_rows, kplace, qseg)
    piece = (
        lax.all_gather(own_block[0], "ctx", axis=0, tiled=True),
        lax.all_gather(own_block[1], "ctx", axis=0, tiled=True),
        lax.all_gather(own_block[2], "ctx", axis=0, tiled=True),
        lax.all_gather(own_block[3], "ctx", axis=0, tiled=True),
    )
    owner = jnp.int32(0) // token_slots
    numer, denom = lax.cond(
        owner <= mine, lambda state: add_keys(piece), lambda state: state, empty
    )
    denom_rows = jnp.transpose(denom, (2, 0, 1))
    safe = jnp.where(live[:, None, None], denom_rows, 1.0)
    result = numer / safe[..., None] * live[:, None, None, None].astype(jnp.float32)
    attention = result.reshape(token_slots, QUERY_HEADS * HEAD_SIZE).astype(jnp.bfloat16)
    verdict = jnp.dot(attention, score_vector, preferred_element_type=jnp.float32)
    loglik = jax.nn.log_sigmoid(verdict)
    onehot = span_ids[0][:, None] == jnp.arange(CAND, dtype=jnp.int32)[None, :]
    sums = jnp.sum(jnp.where(onehot, loglik[:, None], 0.0), axis=0)
    tally = jnp.sum(onehot.astype(jnp.float32), axis=0)
    sums, tally = lax.psum((sums, tally), "ctx")
    return (attention[None], (sums / tally)[None])


def solution(mesh):
    placed = (
        P("dp", "ctx", None),
        P("dp", None),
        P("dp"),
        P("dp", "ctx"),
        P("dp", "ctx"),
        P("dp", None),
        P("dp", None),
        P("dp", None),
        P(),
    )
    return jax.shard_map(
        per_device,
        mesh=mesh,
        in_specs=placed,
        out_specs=(P("dp", "ctx", None), P("dp", None)),
        check_vma=False,
    )
```

profile of v0, /device:TPU:8, one launch (start us, length us, event | category | flops | bytes accessed | tf_op | source)
XLA Modules:
  0.0 375.7 jit_solution(2490414776641406215)
XLA Ops:
  7.2 0.0 copy-start
  7.2 0.0 all-gather.8.cloned.1.call-start
  7.2 0.7 all-gather.8.cloned.1.call-update
  7.9 0.0 all-gather.14.cloned.1.call-start
  8.0 0.7 all-gather.14.cloned.1.call-update
  8.7 0.0 all-gather.12.cloned.1.call-start
  8.7 0.7 all-gather.12.cloned.1.call-update
  9.4 0.0 all-gather.10.cloned.1.call-start
  9.5 1.3 fusion.27
  10.8 0.5 fusion.30
  11.3 0.2 multiply_cosine_fusion
  11.5 38.2 %all-gather.8.cloned.1.call-done = bf16[2560,512]{1,0:T(8,128)(2,1)} async-done(((bf16[160,512]{1,0:T(8,128)(2,1)}), bf16[2560,512]{1,0:T(8,128)(2,1)}) %all-gather.8.cloned.1.call-update) | async-done | bytes 2621456 | tf_op jit(solution)/shard_map/all_gather | solution.py:60
  49.8 3.0 copy.43
  52.8 0.0 copy-done
  52.8 0.8 fusion.24
  53.7 0.0 copy-start.4
  53.7 0.0 copy-start.5
  53.8 0.8 copy.44
  54.5 0.0 all-gather.10.cloned.1.call-update
  54.6 0.0 all-gather.16.cloned.1.call-start
  54.6 34.2 %all-gather.14.cloned.1.call-done = bf16[2560,512]{1,0:T(8,128)(2,1)} async-done(((bf16[160,512]{1,0:T(8,128)(2,1)}), bf16[2560,512]{1,0:T(8,128)(2,1)}) %all-gather.14.cloned.1.call-update) | async-done | bytes 2621456 | tf_op jit(solution)/shard_map/all_gather | solution.py:61
  88.8 2.9 convolution_convert_fusion
  91.7 0.0 all-gather.16.cloned.1.call-update
  91.7 0.0 copy-done.4
  91.7 0.6 reshape.251
  92.4 0.0 copy-done.5
  92.4 43.5 %all-gather = s32[1,2048]{1,0:T(1,128)S(1)} all-gather(s32[1,128]{1,0:T(1,128)S(1)} %copy-done.5), channel_id=2, replica_groups=mesh['dp'=16,'ctx'=16] {'ctx'}, dimensions={1}, use_global_device_ids=true | all-gather | bytes 8704 | tf_op jit(solution)/shard_map/all_gather | solution.py:104
  135.8 1.2 select_bitcast_fusion.1
  137.0 38.0 %all-gather.1 = s32[16,1,128]{2,1,0:T(1,128)S(1)} all-gather(s32[1,1,128]{2,1,0:T(1,128)S(1)} %select_bitcast_fusion.1), channel_id=1, replica_groups=mesh['dp'=16,'ctx'=16] {'ctx'}, dimensions={0}, use_global_device_ids=true | all-gather | bytes 8704 | tf_op jit(solution)/shard_map/all_gather | solution.py:103
  175.0 0.5 iota_add_fusion
  175.5 1.2 fusion.31
  176.7 1.2 iota_compare_fusion.1
  177.9 17.7 %copy.45 = bf16[2560,2560]{1,0:T(8,128)(2,1)} copy(bf16[2560,2560]{0,1:T(8,128)(2,1)} %bitcast.64) | data formatting | bytes 26214400 | tf_op jit(solution)/shard_map/dot_general | solution.py:64
  195.6 6.6 %fusion.22 = f32[128,20,128]{0,2,1:T(8,128)S(1)} fusion(bf16[20,128,2560]{2,1,0:T(8,128)(2,1)} %bitcast.63, bf16[1,128,2560]{2,1,0:T(8,128)(2,1)S(1)} %copy-done), kind=kOutput, calls=%fused_computation.37 | convolution fusion | flops 1677721600 | bytes 15073280 | tf_op jit(solution)/shard_map/dot_general | solution.py:64
  202.2 0.2 multiply_subtract_fusion
  202.4 0.4 copy.47
  202.8 1.5 copy.46
  204.3 0.1 fusion.20
  204.4 2.1 fusion.19
  206.5 24.0 %all-gather.10.cloned.1.call-done = bf16[2048,512]{1,0:T(8,128)(2,1)} async-done(((bf16[128,512]{1,0:T(8,128)(2,1)}), bf16[2048,512]{1,0:T(8,128)(2,1)}) %all-gather.10.cloned.1.call-update) | async-done | bytes 2097168 | tf_op jit(solution)/shard_map/all_gather | solution.py:101
  230.5 59.5 %all-gather.16.cloned.1.call-done = bf16[2048,512]{1,0:T(8,128)(2,1)} async-done(((bf16[128,512]{1,0:T(8,128)(2,1)}), bf16[2048,512]{1,0:T(8,128)(2,1)}) %all-gather.16.cloned.1.call-update) | async-done | bytes 2097168 | tf_op jit(solution)/shard_map/all_gather | solution.py:102
  290.0 32.8 %conditional.1 = (f32[4,5,128]{2,1,0:T(8,128)}, f32[128,4,5,128]{0,3,2,1:T(8,128)S(1)}) conditional(s32[]{:T(128)} %convert_element_type.59, () %tuple.28, (s32[2048]{0:T(1024)S(1)}, s32[1,128]{1,0:T(1,128)S(1)}, s32[2048]{0:T(1024)S(1)}, s32[]{:T(128)}, s32[128]{0:T(128)S(1)}, /*index=5*/s32[128]{0:T(128)S(1)}, s32[]{:T(128)}, s32[]{:T(128)}, ...), branch_computations={%region_4.5_spmd, %region_5.7_spmd.clone.clone} | conditional | flops 2717421312 | bytes 68356152 | solution.py:107
  290.0 0.7 and_select_fusion
  290.7 0.7 add_select_fusion
  291.4 1.9 compare_and_fusion
  293.3 4.0 %reshape.253 = bf16[2048,4,128]{2,1,0:T(4,128)(2,1)} reshape(bf16[2048,512]{1,0:T(8,128)(2,1)} %get-tuple-element.241) | data formatting | bytes 4194304 | tf_op jit(solution)/shard_map/cond/branch_1_fun/reshape | solution.py:80
  297.3 11.2 %fusion = (f32[4,5,128]{2,1,0:T(8,128)}, f32[4,2048,128,5]{2,1,3,0:T(8,128)}) fusion(pred[128,2048]{0,1:T(8,128)(4,1)S(1)} %compare_and_fusion, bf16[128,4,5,128]{3,0,2,1:T(8,128)(2,1)S(1)} %get-tuple-element.242, bf16[2048,4,128,1]{2,1,0,3:T(4,128)(2,1)} %bitcast.72), kind=kOutput, calls=%fused_computation.1 | convolution fusion | flops 1357903360 | bytes 23996416 | tf_op jit(solution)/shard_map/cond/branch_1_fun/qhgd,khd->hgqk/dot_general | solution.py:77
  308.5 0.0 copy-done.2
  308.5 2.1 reshape.254
  310.6 11.9 %fusion.10 = f32[128,4,5,128]{3,0,2,1:T(8,128)S(1)} fusion(bf16[2048,4,128,1]{2,1,0,3:T(4,128)(2,1)} %bitcast.71, f32[4,2048,128,5]{2,1,3,0:T(8,128)} %get-tuple-element.266, pred[128,2048]{0,1:T(8,128)(4,1)S(1)} %compare_and_fusion), kind=kOutput, calls=%fused_computation.10 | convolution fusion | flops 1357905920 | bytes 24641536 | tf_op jit(solution)/shard_map/cond/branch_1_fun/hgqk,khd->qhgd/dot_general | solution.py:87
  322.4 0.4 copy.61
  322.8 0.0 copy-start.3
  322.9 0.0 copy-start.6
  322.9 0.0 copy-start.1
  322.9 0.8 select_bitcast_fusion
  323.7 0.9 multiply_convert_fusion
  324.5 1.1 copy.49
  325.6 0.0 copy-done.3
  325.6 0.2 fusion.29
  325.8 0.0 copy-done.6
  325.8 0.1 convert_reduce_fusion
  326.0 42.6 %all-reduce = (f32[32]{0:T(128)S(1)}, f32[32]{0:T(128)S(1)}) all-reduce(f32[32]{0:T(128)S(1)} %get-tuple-element.260, f32[32]{0:T(128)S(1)} %get-tuple-element.259), channel_id=1, replica_groups=mesh['dp'=16,'ctx'=16] {'ctx'}, use_global_device_ids=true, to_apply=%region_8.9 | all-reduce | flops 64 | bytes 512 | tf_op jit(solution)/shard_map/psum | solution.py:119
  368.6 0.5 divide_bitcast_fusion
  369.1 0.0 copy-done.1
  (11 shorter events, 0.1 us)
Async XLA Ops:
  7.2 45.6 %copy-start = (bf16[1,128,2560]{2,1,0:T(8,128)(2,1)S(1)}, bf16[1,128,2560]{2,1,0:T(8,128)(2,1)}, u32[]{:S(2)}) copy-start(bf16[1,128,2560]{2,1,0:T(8,128)(2,1)} %param.11) | copy-start | bytes 1966084
  7.2 42.6 %all-gather.8.cloned.1.call-start = ((), (), s32[]{:S(2)}) async-start(), calls=%async_computation | async-start | bytes 2785280 | tf_op jit(solution)/shard_map/all_gather | solution.py:60
  7.9 80.9 %all-gather.14.cloned.1.call-start = ((), (), s32[]{:S(2)}) async-start(), calls=%async_computation.3 | async-start | bytes 2785280 | tf_op jit(solution)/shard_map/all_gather | solution.py:61
  8.7 169.2 %all-gather.12.cloned.1.call-start = ((), (), s32[]{:S(2)}) async-start(), calls=%async_computation.2 | async-start | bytes 13926400 | tf_op jit(solution)/shard_map/all_gather | solution.py:59
  9.4 221.1 %all-gather.10.cloned.1.call-start = ((), (), s32[]{:S(2)}) async-start(), calls=%async_computation.1 | async-start | bytes 2228224 | tf_op jit(solution)/shard_map/all_gather | solution.py:101
  53.7 38.0 %copy-start.4 = (bf16[2560]{0:T(1024)(128)(2,1)S(1)}, bf16[2560]{0:T(1024)(128)(2,1)}, u32[]{:S(2)}) copy-start(bf16[2560]{0:T(1024)(128)(2,1)} %param.19) | copy-start | bytes 15364
  53.7 38.6 %copy-start.5 = (s32[1,128]{1,0:T(1,128)S(1)}, s32[1,128]{1,0:T(1,128)}, u32[]{:S(2)}) copy-start(s32[1,128]{1,0:T(1,128)} %param.14) | copy-start | bytes 1540
  54.6 235.5 %all-gather.16.cloned.1.call-start = ((), (), s32[]{:S(2)}) async-start(), calls=%async_computation.4 | async-start | bytes 2228224 | tf_op jit(solution)/shard_map/all_gather | solution.py:102
  297.3 11.2 %copy-start.2 = (bf16[2048,512]{1,0:T(8,128)(2,1)S(1)}, bf16[2048,512]{1,0:T(8,128)(2,1)}, u32[]{:S(2)}) copy-start(bf16[2048,512]{1,0:T(8,128)(2,1)} %get-tuple-element.243) | copy-start | bytes 6291460 | tf_op jit(solution)/shard_map/cond
  322.8 2.8 copy-start.3
  322.9 3.0 copy-start.6
  322.9 46.3 %copy-start.1 = (bf16[1,128,2560]{2,1,0:T(8,128)(2,1)S(1)}, bf16[1,128,2560]{2,1,0:T(8,128)(2,1)}, u32[]{:S(2)}) copy-start(bf16[1,128,2560]{2,1,0:T(8,128)(2,1)} %param.11) | copy-start | bytes 1966084
Sparse Core Ops, SparseCore 0:
  9.8 39.9 all-gather.7
  51.6 37.1 all-gather.13
  90.7 76.7 all-gather.11
  170.3 60.1 all-gather.9
  232.8 57.2 all-gather.15
where the time goes:
time: 376 us
  waiting for transfers between devices  158 us (42%)
  blocking collectives  124 us (33%)
  matrix products  33.7 us (9%)
  local copies, waits for them, and re-layouts  31.5 us (8%)
  other arithmetic  14.1 us (4%)
  between operations  14 us (4%)
    all_gather x1, waiting for transfers between devices, per_device(): lax.all_gather(own_block[1], 'ctx', axis=0, tiled=True)  59.5 us
    all_gather x1, blocking collectives, per_device(): lax.all_gather(own_block[3], 'ctx', axis=0, tiled=True)  43.5 us
    psum x1, blocking collectives, per_device(): sums, tally = lax.psum((sums, tally), 'ctx')  42.6 us
    all_gather x1, waiting for transfers between devices, per_device(): lax.all_gather(key_matrix, 'dp', axis=0, tiled=True)  38.2 us
    all_gather x1, blocking collectives, per_device(): lax.all_gather(own_block[2], 'ctx', axis=0, tiled=True)  38 us
    all_gather x1, waiting for transfers between devices, per_device(): lax.all_gather(value_matrix, 'dp', axis=0, tiled=True)  34.2 us
    all_gather x1, waiting for transfers between devices, per_device(): lax.all_gather(own_block[0], 'ctx', axis=0, tiled=True)  24 us
    dot_general x2, local copies, waits for them, and re-layouts, per_device(): jnp.dot(inputs, piece, preferred_element_type=jnp.float32)  20.7 us
  transfers between devices with their start and end apart: 5, of which 4 were waited for; matrix products, arithmetic and copies ran while one was open for 11% of the time, Pallas kernels for 0%

commit v1 on v0

--- a/solution.py
+++ b/solution.py
@@ -58,7 +58,9 @@
     pieces = (
         lax.all_gather(query_weight, "dp", axis=0, tiled=True),
         lax.all_gather(key_matrix, "dp", axis=0, tiled=True),
-        lax.all_gather(value_matrix, "dp", axis=0, tiled=True),
+        jnp.concatenate(
+            lax.all_to_all(jnp.stack([value_matrix] * lax.axis_size("dp")), "dp", 0, 0), axis=0
+        ),
     )
     query, key_rows, raw_values = tuple(
         (jnp.dot(inputs, piece, preferred_element_type=jnp.float32) for piece in pieces)

time: 376 us -> 356 us (0.947)
  waiting for transfers between devices: 158 us -> 130 us
  starting transfers between devices: 0.19 us -> 6.57 us
  local copies, waits for them, and re-layouts: 31.5 us -> 36.2 us
    all_gather x1 -> x0, waiting for transfers between devices: 34.2 us -> none  [per_device(): lax.all_gather(value_matrix, 'dp', axis=0, tiled=True)]
    all_gather x1, waiting for transfers between devices: 38.2 us -> 49 us  [per_device(): lax.all_gather(key_matrix, 'dp', axis=0, tiled=True)]
    all_to_all x0 -> x1, starting transfers between devices: none -> 6.42 us  [per_device(): lax.all_to_all(jnp.stack([value_matrix] * lax.axis_size('dp')), 'dp', 0, 0)]
    all_gather x1, waiting for transfers between devices: 24 us -> 19.8 us  [per_device(): lax.all_gather(own_block[0], 'ctx', axis=0, tiled=True)]
  transfers between devices with their start and end apart: 5 -> 5, of which waited for: 4 -> 3; matrix products, arithmetic and copies ran while one was open for 11% -> 13% of each run, Pallas kernels for 0% -> 0%
where the time goes in v1:
time: 356 us; the launch traced here: 355 us
  waiting for transfers between devices  130 us (37%)
  blocking collectives  125 us (35%)
  local copies, waits for them, and re-layouts  36.2 us (10%)
  matrix products  32.5 us (9%)
  between operations  14 us (4%)
  other arithmetic  11.2 us (3%)
  starting transfers between devices  6.57 us (2%)
    all_gather x1, waiting for transfers between devices, per_device(): lax.all_gather(own_block[1], 'ctx', axis=0, tiled=True)  59.6 us
    all_gather x1, waiting for transfers between devices, per_device(): lax.all_gather(key_matrix, 'dp', axis=0, tiled=True)  49 us
    all_gather x1, blocking collectives, per_device(): lax.all_gather(own_block[3], 'ctx', axis=0, tiled=True)  44.4 us
    psum x1, blocking collectives, per_device(): sums, tally = lax.psum((sums, tally), 'ctx')  42.7 us
    all_gather x1, blocking collectives, per_device(): lax.all_gather(own_block[2], 'ctx', axis=0, tiled=True)  38 us
    dot_general x2, local copies, waits for them, and re-layouts, per_device(): jnp.dot(inputs, piece, preferred_element_type=jnp.float32)  22 us
    all_gather x1, waiting for transfers between devices, per_device(): lax.all_gather(own_block[0], 'ctx', axis=0, tiled=True)  19.8 us
    dot_general x1, matrix products, add_keys(): jnp.einsum('hgqk,khd->qhgd', weights.astype(jnp.bfloat16), value_portion....  11.3 us
  transfers between devices with their start and end apart: 5, of which 3 were waited for; matrix products, arithmetic and copies ran while one was open for 13% of the time, Pallas kernels for 0%

profile of v1, /device:TPU:8, one launch (start us, length us, event | category | flops | bytes accessed | tf_op | source)
XLA Modules:
  0.0 355.3 jit_solution(7670964878780520455)
XLA Ops:
  7.2 0.0 copy-start
  7.2 0.0 all-gather.7.cloned.1.call-start
  7.2 0.7 all-gather.7.cloned.1.call-update
  7.9 0.0 all-gather.11.cloned.1.call-start
  8.0 0.7 all-gather.11.cloned.1.call-update
  8.7 2.6 stack.2
  11.3 0.0 copy-start.5
  11.3 6.4 %all-to-all-start = ((bf16[16,160,512]{2,1,0:T(8,128)(2,1)}), bf16[16,160,512]{2,1,0:T(8,128)(2,1)S(1)}, u32[]{:S(2)}, u32[]{:S(2)}) async-start(bf16[16,160,512]{2,1,0:T(8,128)(2,1)} %stack.2), calls=%async_computation | async-start | bytes 5242880 | tf_op jit(solution)/shard_map/all_to_all | solution.py:62
  17.7 0.0 all-gather.9.cloned.1.call-start
  17.8 0.0 copy-done.5
  17.8 0.7 fusion.27
  18.5 0.6 fusion.30
  19.1 0.2 multiply_cosine_fusion
  19.3 49.0 %all-gather.7.cloned.1.call-done = bf16[2560,512]{1,0:T(8,128)(2,1)} async-done(((bf16[160,512]{1,0:T(8,128)(2,1)}), bf16[2560,512]{1,0:T(8,128)(2,1)}) %all-gather.7.cloned.1.call-update) | async-done | bytes 2621456 | tf_op jit(solution)/shard_map/all_gather | solution.py:60
  68.3 4.4 %copy.43 = bf16[512,2560]{1,0:T(8,128)(2,1)} copy(bf16[512,2560]{0,1:T(8,128)(2,1)} %bitcast.72) | data formatting | bytes 5242880 | tf_op jit(solution)/shard_map/dot_general | solution.py:66
  72.7 0.0 copy-done
  72.7 2.6 fusion.24
  75.4 0.0 copy-start.3
  75.4 0.0 copy-start.4
  75.4 0.8 copy.44
  76.2 0.0 all-gather.9.cloned.1.call-update
  76.2 0.0 all-gather.13.cloned.1.call-start
  76.3 0.0 all-to-all-done
  76.3 1.2 convolution_convert_fusion
  77.5 0.0 all-gather.13.cloned.1.call-update
  77.5 0.0 copy-done.3
  77.5 0.0 copy-done.4
  77.5 44.4 %all-gather = s32[1,2048]{1,0:T(1,128)S(1)} all-gather(s32[1,128]{1,0:T(1,128)S(1)} %copy-done.4), channel_id=2, replica_groups=mesh['dp'=16,'ctx'=16] {'ctx'}, dimensions={1}, use_global_device_ids=true | all-gather | bytes 8704 | tf_op jit(solution)/shard_map/all_gather | solution.py:106
  121.9 1.2 select_bitcast_fusion.1
  123.1 38.0 %all-gather.1 = s32[16,1,128]{2,1,0:T(1,128)S(1)} all-gather(s32[1,1,128]{2,1,0:T(1,128)S(1)} %select_bitcast_fusion.1), channel_id=1, replica_groups=mesh['dp'=16,'ctx'=16] {'ctx'}, dimensions={0}, use_global_device_ids=true | all-gather | bytes 8704 | tf_op jit(solution)/shard_map/all_gather | solution.py:105
  161.1 0.6 iota_add_fusion
  161.8 0.6 fusion.31
  162.4 0.6 iota_compare_fusion.1
  163.0 0.0 all-gather.11.cloned.1.call-done
  163.0 17.6 %copy.45 = bf16[2560,2560]{1,0:T(8,128)(2,1)} copy(bf16[2560,2560]{0,1:T(8,128)(2,1)} %bitcast.65) | data formatting | bytes 26214400 | tf_op jit(solution)/shard_map/dot_general | solution.py:66
  180.7 6.6 %fusion.22 = f32[128,20,128]{0,2,1:T(8,128)S(1)} fusion(bf16[20,128,2560]{2,1,0:T(8,128)(2,1)} %bitcast.64, bf16[1,128,2560]{2,1,0:T(8,128)(2,1)S(1)} %copy-done), kind=kOutput, calls=%fused_computation.37 | convolution fusion | flops 1677721600 | bytes 15073280 | tf_op jit(solution)/shard_map/dot_general | solution.py:66
  187.3 0.2 multiply_subtract_fusion
  187.5 0.4 copy.47
  187.9 1.5 copy.46
  189.4 0.1 fusion.20
  189.5 2.1 fusion.19
  191.6 19.8 %all-gather.9.cloned.1.call-done = bf16[2048,512]{1,0:T(8,128)(2,1)} async-done(((bf16[128,512]{1,0:T(8,128)(2,1)}), bf16[2048,512]{1,0:T(8,128)(2,1)}) %all-gather.9.cloned.1.call-update) | async-done | bytes 2097168 | tf_op jit(solution)/shard_map/all_gather | solution.py:103
  211.4 59.6 %all-gather.13.cloned.1.call-done = bf16[2048,512]{1,0:T(8,128)(2,1)} async-done(((bf16[128,512]{1,0:T(8,128)(2,1)}), bf16[2048,512]{1,0:T(8,128)(2,1)}) %all-gather.13.cloned.1.call-update) | async-done | bytes 2097168 | tf_op jit(solution)/shard_map/all_gather | solution.py:104
  271.0 32.9 %conditional.1 = (f32[4,5,128]{2,1,0:T(8,128)S(1)}, f32[128,4,5,128]{0,3,2,1:T(8,128)S(1)}) conditional(s32[]{:T(128)} %convert_element_type.59, () %tuple.28, (s32[2048]{0:T(1024)S(1)}, s32[1,128]{1,0:T(1,128)S(1)}, s32[2048]{0:T(1024)S(1)}, s32[]{:T(128)}, s32[128]{0:T(128)S(1)}, /*index=5*/s32[128]{0:T(128)S(1)}, s32[]{:T(128)}, ...), branch_computations={%region_4.5_spmd, %region_5.7_spmd.clone.clone} | conditional | flops 2717421312 | bytes 68356152 | solution.py:109
  271.0 0.7 and_select_fusion
  271.6 0.7 add_select_fusion
  272.3 1.9 compare_and_fusion
  274.2 4.0 %reshape.259 = bf16[2048,4,128]{2,1,0:T(4,128)(2,1)} reshape(bf16[2048,512]{1,0:T(8,128)(2,1)} %get-tuple-element.241) | data formatting | bytes 4194304 | tf_op jit(solution)/shard_map/cond/branch_1_fun/reshape | solution.py:82
  278.2 0.0 copy-start.2
  278.2 10.6 %fusion = (f32[4,5,128]{2,1,0:T(8,128)S(1)}, f32[4,2048,128,5]{2,1,3,0:T(8,128)}) fusion(pred[128,2048]{0,1:T(8,128)(4,1)S(1)} %compare_and_fusion, bf16[128,4,5,128]{3,0,2,1:T(8,128)(2,1)S(1)} %get-tuple-element.242, bf16[2048,4,128,1]{2,1,0,3:T(4,128)(2,1)} %bitcast.74), kind=kOutput, calls=%fused_computation.1 | convolution fusion | flops 1357903360 | bytes 23996416 | tf_op jit(solution)/shard_map/cond/branch_1_fun/qhgd,khd->hgqk/dot_general | solution.py:79
  288.8 0.0 copy-done.2
  288.9 2.1 reshape.260
  290.9 11.3 %fusion.10 = f32[128,4,5,128]{3,0,2,1:T(8,128)} fusion(bf16[2048,4,128,1]{2,1,0,3:T(4,128)(2,1)} %bitcast.73, f32[4,2048,128,5]{2,1,3,0:T(8,128)} %get-tuple-element.266, pred[128,2048]{0,1:T(8,128)(4,1)S(1)} %compare_and_fusion), kind=kOutput, calls=%fused_computation.10 | convolution fusion | flops 1357905920 | bytes 24641536 | tf_op jit(solution)/shard_map/cond/branch_1_fun/hgqk,khd->qhgd/dot_general | solution.py:89
  302.2 1.7 copy.61
  303.9 0.0 copy-start.6
  303.9 0.0 copy-start.1
  303.9 0.2 multiply_convert_fusion
  304.1 1.1 copy.49
  305.2 0.2 fusion.29
  305.4 0.0 copy-done.6
  305.4 0.1 convert_reduce_fusion
  305.5 42.7 %all-reduce = (f32[32]{0:T(128)S(1)}, f32[32]{0:T(128)S(1)}) all-reduce(f32[32]{0:T(128)S(1)} %get-tuple-element.260, f32[32]{0:T(128)S(1)} %get-tuple-element.259), channel_id=1, replica_groups=mesh['dp'=16,'ctx'=16] {'ctx'}, use_global_device_ids=true, to_apply=%region_8.9 | all-reduce | flops 64 | bytes 512 | tf_op jit(solution)/shard_map/psum | solution.py:121
  348.2 0.5 divide_bitcast_fusion
  348.7 0.0 copy-done.1
  (11 shorter events, 0.1 us)
Async XLA Ops:
  7.2 65.6 %copy-start = (bf16[1,128,2560]{2,1,0:T(8,128)(2,1)S(1)}, bf16[1,128,2560]{2,1,0:T(8,128)(2,1)}, u32[]{:S(2)}) copy-start(bf16[1,128,2560]{2,1,0:T(8,128)(2,1)} %param.11) | copy-start | bytes 1966084
  7.2 61.2 %all-gather.7.cloned.1.call-start = ((), (), s32[]{:S(2)}) async-start(), calls=%async_computation.1 | async-start | bytes 2785280 | tf_op jit(solution)/shard_map/all_gather | solution.py:60
  7.9 155.1 %all-gather.11.cloned.1.call-start = ((), (), s32[]{:S(2)}) async-start(), calls=%async_computation.3 | async-start | bytes 13926400 | tf_op jit(solution)/shard_map/all_gather | solution.py:59
  11.3 6.5 %copy-start.5 = (s32[1,16]{1,0:T(1,128)S(1)}, s32[1,16]{1,0:T(1,128)}, u32[]{:S(2)}) copy-start(s32[1,16]{1,0:T(1,128)} %param.12) | copy-start | bytes 196
  11.3 65.0 %all-to-all-start = ((bf16[16,160,512]{2,1,0:T(8,128)(2,1)}), bf16[16,160,512]{2,1,0:T(8,128)(2,1)S(1)}, u32[]{:S(2)}, u32[]{:S(2)}) async-start(bf16[16,160,512]{2,1,0:T(8,128)(2,1)} %stack.2), calls=%async_computation | async-start | bytes 5242880 | tf_op jit(solution)/shard_map/all_to_all | solution.py:62
  17.7 193.7 %all-gather.9.cloned.1.call-start = ((), (), s32[]{:S(2)}) async-start(), calls=%async_computation.2 | async-start | bytes 2228224 | tf_op jit(solution)/shard_map/all_gather | solution.py:103
  75.4 2.1 copy-start.3
  75.4 2.1 copy-start.4
  76.2 194.7 %all-gather.13.cloned.1.call-start = ((), (), s32[]{:S(2)}) async-start(), calls=%async_computation.4 | async-start | bytes 2228224 | tf_op jit(solution)/shard_map/all_gather | solution.py:104
  278.2 10.7 %copy-start.2 = (bf16[2048,512]{1,0:T(8,128)(2,1)S(1)}, bf16[2048,512]{1,0:T(8,128)(2,1)}, u32[]{:S(2)}) copy-start(bf16[2048,512]{1,0:T(8,128)(2,1)} %get-tuple-element.243) | copy-start | bytes 6291460 | tf_op jit(solution)/shard_map/cond
  303.9 1.5 copy-start.6
  303.9 44.8 %copy-start.1 = (bf16[1,128,2560]{2,1,0:T(8,128)(2,1)S(1)}, bf16[1,128,2560]{2,1,0:T(8,128)(2,1)}, u32[]{:S(2)}) copy-start(bf16[1,128,2560]{2,1,0:T(8,128)(2,1)} %param.11) | copy-start | bytes 1966084
Sparse Core Ops, SparseCore 0:
  9.8 58.4 all-gather.6
  70.2 78.0 all-gather.10
  151.3 60.1 all-gather.8
  213.7 57.2 all-gather.12
